TPU v7x, 256 devices: a whole 4x4x8 slice. The times are simulated.
256 devices in a mesh: req: 64 (over z, x, core), tp: 4 (over y).
Axes of the slice: x: 4, y: 4, z: 8, core: 2. Of those that a mesh axis runs over, the one named last changes fastest.
Arguments:
- layer_in: bfloat16 [8192, 2880], P('req', 'tp'), may hold values from -6 to 6
- queries: bfloat16 [8192, 4096], P('req', 'tp'), may hold values from -32 to 32
- key_values: bfloat16 [8192, 2, 512], P('req', None, 'tp'), may hold values from -12 to 12
- prefix_cache: bfloat16 [4, 1024, 2, 512], P(None, 'req', None, 'tp'), may hold values from -8 to 8
- sink_logits: float32 [64], P('tp'), may hold values from 8 to 12
- lengths: int32 [512], P('req'), may hold values from 1 to 16
- groups: int32 [512], P('req'), may hold values from 0 to 3
- batch_home: int32 [64], replicated, may hold values from 0 to 63, each once
- expert_ids: int32 [8192, 4], P('req'), may hold values from 0 to 31, all different within a row; in each aligned block of 128 rows (0 to 127, 128 to 255, ...) at most 24 rows name the same one
- router_logits: float32 [8192, 4], P('req'), may hold values from -6 to 6
- norm_gain: float32 [2880], replicated, may hold values from 0.1 to 1.9
- output_weight: bfloat16 [4096, 2880], P('tp'), may hold values from -0.09375 to 0.09375
- gate_up: bfloat16 [64, 2880, 2, 1440], P('req', None, None, 'tp'), may hold values from -0.109375 to 0.109375
- expert_down: bfloat16 [64, 1440, 2880], P('req', 'tp'), may hold values from -0.109375 to 0.109375
Outputs:
- layer_out: bfloat16 [8192, 2880], P('req', 'tp')
Inputs may be any that keep to these rules, and one draw needn't show every extreme that they name: `expert_ids`: in the token slots of one index of req, no expert is named by more than 24 slots. `batch_home`: A permutation.
All inputs are finite; a program needn't handle non-finite values.
Results may differ from a plain program's by a relative error of at most 0.017.
Values may be sent and summed in bfloat16 or wider, within the bound.
No kernel may reach another device: no remote copies, remote signals or barrier semaphores. Data moves between devices by JAX's collectives and lax.ppermute only.
A program may use at most 192 MiB of HBM per device.

v0:
```python
import jax
import jax.numpy as jnp
from jax import lax
from jax.sharding import PartitionSpec as P

D = 2880
HD = 64
EXPERTS = 32
TOPK = 4
PREFIX = 1024
CAP = 24
theta_base = 150000.0
norm_eps = 1e-05
logit_scale = 0.125
masked_score = -1e30


def rotate(values, positions):
    middle = values.shape[-1] // 2
    lane_index = jnp.arange(middle, dtype=jnp.int32).astype(jnp.float32)
    inverse_freq = theta_base ** (-2.0 * lane_index / values.shape[-1])
    angles = positions.astype(jnp.float32)[:, None] * inverse_freq[None, :]
    cosine = jnp.cos(angles)[:, None, :]
    sine_part = jnp.sin(angles)[:, None, :]
    front_half = values[..., :middle]
    back_half = values[..., middle:]
    return jnp.concatenate(
        [front_half * cosine - back_half * sine_part, back_half * cosine + front_half * sine_part],
        axis=-1,
    )


def absorb_block(softmax_state, query_groups, block_keys, block_values, allowed):
    run_max, run_sum, run_acc = softmax_state
    score_matrix = (
        jnp.einsum(
            "rskgd,rbkd->rskgb", query_groups, block_keys, preferred_element_type=jnp.float32
        )
        * logit_scale
    )
    if allowed is not None:
        score_matrix = jnp.where(allowed, score_matrix, masked_score)
    new_max = jnp.maximum(run_max, jnp.max(score_matrix, axis=-1))
    rescale = jnp.exp(run_max - new_max)
    weights = jnp.exp(score_matrix - new_max[..., None])
    new_sum = run_sum * rescale + jnp.sum(weights, axis=-1)
    new_acc = run_acc * rescale[..., None] + jnp.einsum(
        "rskgb,rbkd->rskgd",
        weights.astype(jnp.bfloat16),
        block_values,
        preferred_element_type=jnp.float32,
    )
    return (new_max, new_sum, new_acc)


def body(
    layer_in,
    queries,
    key_values,
    prefix_cache,
    sink_logits,
    lengths,
    groups,
    batch_home,
    expert_ids,
    router_logits,
    norm_gain,
    output_weight,
    gate_up,
    expert_down,
):
    tokens = queries.shape[0]
    requests = lengths.shape[0]
    suffix = tokens // requests
    local_heads = sink_logits.shape[0]
    kv_local = key_values.shape[2] // HD
    per_group = local_heads // kv_local
    slot_index = jnp.tile(jnp.arange(suffix, dtype=jnp.int32), requests)
    positions = PREFIX + slot_index
    rotated_queries = rotate(
        queries.reshape(tokens, local_heads, HD).astype(jnp.float32), positions
    ).astype(jnp.bfloat16)
    query_groups = rotated_queries.reshape(requests, suffix, kv_local, per_group, HD)
    fresh_keys = rotate(
        key_values[:, 0].reshape(tokens, kv_local, HD).astype(jnp.float32), positions
    ).astype(jnp.bfloat16)
    fresh_keys = fresh_keys.reshape(requests, suffix, kv_local, HD)
    fresh_values = key_values[:, 1].reshape(requests, suffix, kv_local, HD)
    sink_values = sink_logits.reshape(kv_local, per_group)
    state_shape = (requests, suffix, kv_local, per_group)
    start_state = (
        jnp.broadcast_to(sink_values[None, None], state_shape),
        jnp.ones(state_shape, jnp.float32),
        jnp.zeros(state_shape + (HD,), jnp.float32),
    )
    page_rows = lax.all_gather(prefix_cache, "req", axis=1, tiled=True)
    span_rows = page_rows.shape[1]
    block_rows = 512
    chosen = page_rows[groups]
    stacked = chosen.reshape(requests, span_rows // block_rows, block_rows, 2, kv_local, HD)

    def absorb_one(inner_state, block_index):
        block_pair = lax.dynamic_index_in_dim(stacked, block_index, 1, keepdims=False)
        return (
            absorb_block(inner_state, query_groups, block_pair[:, :, 0], block_pair[:, :, 1], None),
            None,
        )

    final_state, _ = lax.scan(absorb_one, start_state, jnp.arange(span_rows // block_rows))
    local_pos = jnp.arange(suffix, dtype=jnp.int32)
    causal = local_pos[None, :] <= local_pos[:, None]
    within = local_pos[None, None, :] < lengths[:, None, None]
    allowed = (causal[None] & within)[:, :, None, None, :]
    run_max, run_sum, run_acc = absorb_block(
        final_state, query_groups, fresh_keys, fresh_values, allowed
    )
    attention = (
        (run_acc / run_sum[..., None]).reshape(tokens, local_heads * HD).astype(jnp.bfloat16)
    )
    partial_value = jnp.dot(attention, output_weight, preferred_element_type=jnp.float32)
    tp_index = lax.axis_index("tp")
    quarter_cols = D // lax.axis_size("tp")
    placed = lax.dynamic_update_slice_in_dim(
        jnp.zeros((tokens, D), jnp.float32),
        layer_in.astype(jnp.float32),
        tp_index * quarter_cols,
        1,
    )
    residual = lax.psum((partial_value + placed).astype(jnp.bfloat16), "tp")
    live_rows = slot_index < jnp.repeat(lengths, suffix)
    pair_weight = jnp.where(live_rows[:, None], jax.nn.softmax(router_logits, axis=-1), 0.0).astype(
        jnp.bfloat16
    )
    flat_ids = expert_ids.reshape(-1)
    onehot = (flat_ids[:, None] == jnp.arange(EXPERTS, dtype=jnp.int32)[None, :]).astype(jnp.int32)
    before = jnp.cumsum(onehot, axis=0) - onehot
    rank_in = jnp.sum(before * onehot, axis=1)
    flat_slot = flat_ids * CAP + rank_in
    pair_token = jnp.arange(tokens * TOPK, dtype=jnp.int32) // TOPK
    token_table = (
        jnp.full((EXPERTS * CAP,), tokens, dtype=jnp.int32)
        .at[flat_slot]
        .set(pair_token)
        .reshape(EXPERTS, CAP)
    )
    weight_table = (
        jnp.zeros((EXPERTS * CAP,), jnp.bfloat16)
        .at[flat_slot]
        .set(pair_weight.reshape(-1))
        .reshape(EXPERTS, CAP)
    )
    devices_req = lax.axis_size("req")
    slab_count = gate_up.shape[0]
    split_count = devices_req * slab_count // EXPERTS
    slab_ids = jnp.arange(devices_req * slab_count, dtype=jnp.int32).reshape(
        devices_req, slab_count
    )
    expert_of = slab_ids // split_count
    token_send = token_table[expert_of]
    weight_send = weight_table[expert_of]
    padded = jnp.concatenate([residual, jnp.zeros((1, residual.shape[1]), jnp.bfloat16)], axis=0)
    rows_send = padded[token_send]
    device_range = jnp.arange(devices_req, dtype=jnp.int32)
    inverse = jnp.sum(
        device_range[:, None] * (batch_home[:, None] == device_range[None, :]).astype(jnp.int32),
        axis=0,
    )
    first_copy = (
        (lax.axis_index("req") * slab_count + jnp.arange(slab_count, dtype=jnp.int32)) % split_count
        == 0
    ).astype(jnp.float32)
    rows_in = lax.all_to_all(rows_send, "req", split_axis=0, concat_axis=0, tiled=True)
    arrived_weight = lax.all_to_all(weight_send, "req", split_axis=0, concat_axis=0, tiled=True)
    arrived_token = lax.all_to_all(token_send, "req", split_axis=0, concat_axis=0, tiled=True)
    rows_float = rows_in.astype(jnp.float32)
    row_scale = lax.rsqrt(jnp.mean(rows_float * rows_float, axis=-1, keepdims=True) + norm_eps)
    normed = (rows_float * row_scale * norm_gain).astype(jnp.bfloat16)
    gate_and_up = jnp.einsum(
        "njcd,jdgf->njcgf", normed, gate_up, preferred_element_type=jnp.float32
    )
    hidden = (jax.nn.silu(gate_and_up[..., 0, :]) * gate_and_up[..., 1, :]).astype(jnp.bfloat16)
    partial_out = jnp.einsum(
        "njcf,jfd->njcd", hidden, expert_down, preferred_element_type=jnp.float32
    )
    value_total = lax.psum_scatter(
        partial_out.astype(jnp.bfloat16), "tp", scatter_dimension=3, tiled=True
    ).astype(jnp.float32)
    own_rows = lax.dynamic_slice_in_dim(rows_float, tp_index * quarter_cols, quarter_cols, 3)
    result = (
        arrived_weight.astype(jnp.float32)[..., None]
        * (value_total + first_copy[None, :, None, None] * own_rows)
    ).astype(jnp.bfloat16)
    moved = result[inverse]
    moved_token = arrived_token[inverse]
    returned = lax.all_to_all(moved, "req", split_axis=0, concat_axis=0, tiled=True)
    returned_token = lax.all_to_all(moved_token, "req", split_axis=0, concat_axis=0, tiled=True)
    flat_rows = returned.reshape(-1, quarter_cols)
    flat_token = returned_token.reshape(-1)
    selector = (jnp.arange(tokens, dtype=jnp.int32)[:, None] == flat_token[None, :]).astype(
        jnp.bfloat16
    )
    return jnp.dot(selector, flat_rows, preferred_element_type=jnp.float32).astype(jnp.bfloat16)


def solution(mesh):
    placed = (
        P("req", "tp"),
        P("req", "tp"),
        P("req", None, "tp"),
        P(None, "req", None, "tp"),
        P("tp"),
        P("req"),
        P("req"),
        P(),
        P("req", None),
        P("req", None),
        P(),
        P("tp", None),
        P("req", None, None, "tp"),
        P("req", "tp", None),
    )
    return jax.shard_map(
        body, mesh=mesh, in_specs=placed, out_specs=P("req", "tp"), check_vma=False
    )
```

profile of v0, /device:TPU:2, one launch (start us, length us, event | category | flops | bytes accessed | tf_op | source)
XLA Modules:
  0.0 776.3 jit_solution(6258052218255485450)
XLA Ops:
  8.5 1.8 copy.74
  12.2 2.1 copy.75
  14.3 2.0 copy.77
  17.4 2.0 copy.78
  20.8 1.5 reshape_squeeze.4
  24.1 1.5 pad_maximum_fusion
  26.4 2.4 fusion.60
  28.8 56.3 %all-gather.2.cloned.1.call-done = bf16[4,1024,2,128]{3,2,1,0:T(2,128)(2,1)} async-done(((bf16[4,16,2,128]{3,2,1,0:T(2,128)(2,1)}), bf16[4,1024,2,128]{3,2,1,0:T(2,128)(2,1)}) %all-gather.2.cloned.1.call-update) | async-done | bytes 2097168 | tf_op jit(solution)/shard_map/all_gather | solution.py:96
  85.1 11.4 %gather_fusion.3 = bf16[8,1024,2,128]{3,2,1,0:T(2,128)(2,1)} fusion(bf16[4,1024,2,128]{3,2,1,0:T(2,128)(2,1)} %all-gather.2.cloned.1.call-done, s32[1024]{0:T(1024)S(1)} %pad_clamp_fusion.1), kind=kCustom, calls=%fused_computation.3 | custom fusion | bytes 8388640 | tf_op jit(solution)/shard_map/gather | solution.py:99
  96.5 17.5 %reshape.462 = bf16[8,2,512,2,2,64]{5,4,3,2,1,0:T(2,128)(2,1)} reshape(bf16[8,1024,2,128]{3,2,1,0:T(2,128)(2,1)} %gather_fusion.3) | data formatting | bytes 8388608 | tf_op jit(solution)/shard_map/reshape | solution.py:100
  114.0 20.0 %copy.79 = bf16[8,2,512,2,2,64]{2,5,4,0,3,1:T(8,128)(2,1)} copy(bf16[8,2,512,2,2,64]{5,4,3,2,1,0:T(2,128)(2,1)} %reshape.462) | data formatting | bytes 8388608
  134.1 26.8 %while.15 = (s32[]{:T(128)}, f32[8,16,2,8]{1,3,2,0:T(8,128)S(1)}, f32[8,16,2,8]{1,3,2,0:T(8,128)S(1)}, f32[8,16,2,8,64]{4,1,3,2,0:T(8,128)S(1)}, s32[2]{0:T(128)...) while((s32[]{:T(128)}, f32[8,16,2,8]{1,3,2,0:T(8,128)S(1)}, ...), condition=%wide.region_11.12_spmd.clone, body=%wide.region_8.11_spmd.clone.sunk | while | flops 277223424 | bytes 46792948 | solution.py:109
  136.9 1.9 dynamic-slice_bitcast_fusion.2
  138.8 1.3 copy-done.2
  140.9 1.9 copy-done.1
  144.1 3.4 fusion.76
  150.3 1.9 dynamic-slice_bitcast_fusion.2
  154.3 1.9 copy-done.1
  157.4 3.4 fusion.76
  160.9 1.6 fusion.38
  162.5 2.0 fusion.35
  165.1 4.4 fusion.61
  170.6 2.6 scatter_custom_fusion
  175.4 43.8 %all-reduce.3.cloned.1.call-done = bf16[128,2880]{0,1:T(8,128)(2,1)} async-done(((bf16[128,2880]{0,1:T(8,128)(2,1)}), bf16[128,2880]{0,1:T(8,128)(2,1)}) %all-reduce.3.cloned.1.call-update) | async-done | bytes 737296 | tf_op jit(solution)/shard_map/psum | solution.py:129
  219.3 2.3 copy.108
  222.7 8.1 %gather_fusion.4 = bf16[1536,2880]{1,0:T(8,128)(2,1)} fusion(bf16[129,2880]{1,0:T(8,128)(2,1)S(1)} %concatenate.27.clone, s32[2048]{0:T(1024)S(1)} %pad_clamp_fusion), kind=kCustom, calls=%fused_computation.4 | custom fusion | bytes 17700864 | tf_op jit(solution)/shard_map/gather | solution.py:162
  230.8 210.6 %all_to_all.25 = bf16[64,1,24,2880]{3,2,1,0:T(8,128)(2,1)S(1)} all-to-all(bf16[64,1,24,2880]{3,2,1,0:T(8,128)(2,1)} %bitcast.180), channel_id=1, replica_groups=mesh['req'=64,'tp'=4] {'req'}, dimensions={0} | all-to-all | bytes 17694720 | tf_op jit(solution)/shard_map/all_to_all | solution.py:172
  441.5 1.9 multiply_reduce_fusion
  443.3 1.6 copy-done.3
  444.9 10.1 %fusion.25 = f32[64,1,24,2,360]{4,2,3,0,1:T(8,128)S(1)} fusion(bf16[1,2880,2,360]{1,3,2,0:T(8,128)(2,1)} %param.28, f32[2880]{0:T(1024)S(1)} %copy-done.12, f32[64,24]{1,0:T(8,128)S(1)} %add_rsqrt_fusion, bf16[64,1,24,2880]{3,2,1,0:T(8,128)(2,1)S(1)} %all_to_all.25), kind=kOutput, calls=%fused_computation.40 | convolution fusion | flops 6387793920 | bytes 17435904 | tf_op jit(solution)/shard_map/njcd,jdgf->njcgf/dot_general | solution.py:178
  455.1 7.7 convert_bitcast_fusion
  462.8 42.9 %copy.105 = bf16[64,1,24,2880]{2,0,1,3:T(8,128)(2,1)} copy(bf16[64,1,24,2880]{3,2,0,1:T(8,128)(2,1)} %convert_bitcast_fusion) | data formatting | bytes 17694720
  505.7 64.7 %reshape.463 = bf16[2880,1536]{1,0:T(8,128)(2,1)} reshape(bf16[2880,1,64,24]{3,2,1,0:T(8,128)(2,1)} %bitcast.178) | data formatting | bytes 17694720
  571.4 3.8 scatter_custom_fusion.1
  576.6 5.8 all-to-all-start.2
  582.5 8.5 %all-to-all-done.2 = bf16[64,1,24]{2,1,0:T(2,128)(2,1)S(1)} async-done(((bf16[64,1,24]{2,1,0:T(2,128)(2,1)}), bf16[64,1,24]{2,1,0:T(2,128)(2,1)S(1)}, u32[]{:S(2)}, u32[]{:S(2)}) %all-to-all-start.2) | async-done | bytes 3104 | tf_op jit(solution)/shard_map/all_to_all | solution.py:173
  591.0 5.5 all-to-all-start
  596.6 8.6 %all-to-all-done = s32[64,1,24]{2,1,0:T(1,128)S(1)} async-done(((s32[64,1,24]{2,1,0:T(1,128)}), s32[64,1,24]{2,1,0:T(1,128)S(1)}, u32[]{:S(2)}, u32[]{:S(2)}) %all-to-all-start) | async-done | bytes 6176 | tf_op jit(solution)/shard_map/all_to_all | solution.py:174
  606.4 5.9 all-to-all-start.1
  612.2 11.4 %convert_element_type.160 = f32[64,1,24,2880]{3,2,1,0:T(8,128)} convert(bf16[64,1,24,2880]{3,2,1,0:T(8,128)(2,1)} %copy-done.3) | non-fusion elementwise | flops 4423680 | bytes 26542080 | tf_op jit(solution)/shard_map/convert_element_type | solution.py:175
  623.7 29.6 %reduce-scatter.4.cloned.1.call-done = bf16[720,1536]{1,0:T(8,128)(2,1)} async-done(((bf16[2880,1536]{1,0:T(8,128)(2,1)}), bf16[720,1536]{1,0:T(8,128)(2,1)}) %reduce-scatter.4.cloned.1.call-update) | async-done | bytes 2211856
  653.3 21.0 %reshape.464 = bf16[720,1,64,24]{3,2,1,0:T(8,128)(2,1)} reshape(bf16[720,1536]{1,0:T(8,128)(2,1)} %reduce-scatter.4.cloned.1.call-done) | data formatting | bytes 4423680
  674.3 14.0 %copy.106 = bf16[64,1,24,720]{3,2,0,1:T(8,128)(2,1)} copy(bf16[64,1,24,720]{2,0,1,3:T(8,128)(2,1)} %bitcast.179) | data formatting | bytes 4423680
  688.2 6.4 fusion.23
  694.6 3.8 gather_fusion.5
  698.4 10.7 %all-to-all-start.4 = ((bf16[64,1,24,720]{3,2,1,0:T(8,128)(2,1)}), bf16[64,1,24,720]{3,2,1,0:T(8,128)(2,1)}, u32[]{:S(2)}, u32[]{:S(2)}) async-start(bf16[64,1,24,720]{3,2,1,0:T(8,128)(2,1)} %bitcast.181), calls=%async_computation.4 | async-start | bytes 4718592 | tf_op jit(solution)/shard_map/all_to_all | solution.py:195
  710.5 55.5 %all-to-all-done.4 = bf16[64,1,24,720]{3,2,1,0:T(8,128)(2,1)} async-done(((bf16[64,1,24,720]{3,2,1,0:T(8,128)(2,1)}), bf16[64,1,24,720]{3,2,1,0:T(8,128)(2,1)}, u32[]{:S(2)}, u32[]{:S(2)}) %all-to-all-start.4) | async-done | bytes 2211872 | tf_op jit(solution)/shard_map/all_to_all | solution.py:195
  765.9 3.4 convolution_convert_fusion
  (124 shorter events, 25.6 us)
Async XLA Ops:
  6.5 448.5 %copy-start = (bf16[1,360,2880]{2,1,0:T(8,128)(2,1)S(1)}, bf16[1,360,2880]{2,1,0:T(8,128)(2,1)}, u32[]{:S(2)}) copy-start(bf16[1,360,2880]{2,1,0:T(8,128)(2,1)} %param.29) | copy-start | bytes 6220804
  6.5 17.1 %copy-start.9 = (s32[128,4]{0,1:T(4,128)S(1)}, s32[128,4]{0,1:T(4,128)}, u32[]{:S(2)}) copy-start(s32[128,4]{0,1:T(4,128)} %param.24) | copy-start | bytes 6148
  6.5 12.9 %copy-start.6 = (bf16[128,2,128]{2,1,0:T(2,128)(2,1)S(1)}, bf16[128,2,128]{2,1,0:T(2,128)(2,1)}, u32[]{:S(2)}) copy-start(bf16[128,2,128]{2,1,0:T(2,128)(2,1)} %param.18) | copy-start | bytes 196612
  6.5 14.1 %copy-start.13 = (f32[16]{0:T(128)S(1)}, f32[16]{0:T(128)}, u32[]{:S(2)}) copy-start(f32[16]{0:T(128)} %param.20) | copy-start | bytes 196
  6.5 17.4 %copy-start.14 = (s32[8]{0:T(128)S(1)}, s32[8]{0:T(128)}, u32[]{:S(2)}) copy-start(s32[8]{0:T(128)} %param.22) | copy-start | bytes 100
  6.5 78.6 %all-gather.2.cloned.1.call-start = ((), (), s32[]{:S(2)}) async-start(), calls=%async_computation.6 | async-start | bytes 2129920 | tf_op jit(solution)/shard_map/all_gather | solution.py:96
  7.3 212.0 %all-reduce.3.cloned.1.call-start = ((), (), s32[]{:S(2)}) async-start(), calls=%async_computation.7 | async-start | bytes 1474560 | tf_op jit(solution)/shard_map/psum | solution.py:129
  8.4 17.1 %copy-start.15 = (s32[8]{0:T(128)S(1)}, s32[8]{0:T(128)}, u32[]{:S(2)}) copy-start(s32[8]{0:T(128)} %param.21) | copy-start | bytes 100
  25.6 0.8 copy-start.4
  25.7 0.6 copy-start.10
  136.9 3.2 copy-start.5
  138.8 1.3 copy-start.2
  140.8 1.9 copy-start.1
  150.3 3.2 copy-start.5
  152.1 1.3 copy-start.2
  154.2 1.9 copy-start.1
  165.1 4.4 copy-start.7
  170.6 482.7 %reduce-scatter.4.cloned.1.call-start = ((), (), s32[]{:S(2)}) async-start(), calls=%async_computation.8 | async-start | bytes 11059200
  441.5 3.4 copy-start.3
  441.5 3.4 copy-start.12
  570.4 0.6 copy-start.11
  570.4 0.7 copy-start.8
  570.4 12.0 %copy-start.16 = (s32[64]{0:T(128)S(1)}, s32[64]{0:T(128)}, u32[]{:S(2)}) copy-start(s32[64]{0:T(128)} %param.23) | copy-start | bytes 772
  576.6 14.4 %all-to-all-start.2 = ((bf16[64,1,24]{2,1,0:T(2,128)(2,1)}), bf16[64,1,24]{2,1,0:T(2,128)(2,1)S(1)}, u32[]{:S(2)}, u32[]{:S(2)}) async-start(bf16[64,1,24]{2,1,0:T(2,128)(2,1)} %copy.72), calls=%async_computation.2 | async-start | bytes 65536 | tf_op jit(solution)/shard_map/all_to_all | solution.py:173
  591.0 14.2 %all-to-all-start = ((s32[64,1,24]{2,1,0:T(1,128)}), s32[64,1,24]{2,1,0:T(1,128)S(1)}, u32[]{:S(2)}, u32[]{:S(2)}) async-start(s32[64,1,24]{2,1,0:T(1,128)} %bitcast.5), calls=%async_computation | async-start | bytes 65536 | tf_op jit(solution)/shard_map/all_to_all | solution.py:174
  606.4 92.1 %all-to-all-start.1 = ((s32[64,1,24]{2,1,0:T(1,128)}), s32[64,1,24]{2,1,0:T(1,128)S(1)}, u32[]{:S(2)}, u32[]{:S(2)}) async-start(s32[64,1,24]{2,1,0:T(1,128)} %bitcast.10), calls=%async_computation.1 | async-start | bytes 65536 | tf_op jit(solution)/shard_map/all_to_all | solution.py:196
  698.4 67.5 %all-to-all-start.4 = ((bf16[64,1,24,720]{3,2,1,0:T(8,128)(2,1)}), bf16[64,1,24,720]{3,2,1,0:T(8,128)(2,1)}, u32[]{:S(2)}, u32[]{:S(2)}) async-start(bf16[64,1,24,720]{3,2,1,0:T(8,128)(2,1)} %bitcast.181), calls=%async_computation.4 | async-start | bytes 4718592 | tf_op jit(solution)/shard_map/all_to_all | solution.py:195
Sparse Core Ops, SparseCore 0:
  10.0 75.0 all-gather.1
  170.7 48.5 all-reduce.2
  570.5 82.6 reduce-scatter.3
where the time goes:
time: 791 us; the launch traced here: 776 us
  local copies, waits for them, and re-layouts  246 us (31%)
  blocking collectives  211 us (27%)
  waiting for transfers between devices  203 us (26%)
  matrix products  38.4 us (5%)
  other arithmetic  31.5 us (4%)
  starting transfers between devices  28 us (4%)
  between operations  14 us (2%)
    all_to_all x1, blocking collectives, body(): lax.all_to_all(rows_send, 'req', split_axis=0, concat_axis=0, tiled=True)  211 us
    unnamed x37, local copies, waits for them, and re-layouts  170 us
    all_gather x1, waiting for transfers between devices, body(): page_rows = lax.all_gather(prefix_cache, 'req', axis=1, tiled=True)  56.3 us
    all_to_all x1, waiting for transfers between devices, body(): lax.all_to_all(moved, 'req', split_axis=0, concat_axis=0, tiled=True)  55.5 us
    psum x1, waiting for transfers between devices, body(): residual = lax.psum((partial_value + placed).astype(jnp.bfloat16), 'tp')  43.8 us
    unnamed x4, waiting for transfers between devices  30.3 us
    reshape x1, local copies, waits for them, and re-layouts, body(): chosen.reshape(requests, span_rows // block_rows, block_rows, 2, kv_local...  17.5 us
  transfers between devices with their start and end apart: 7, of which 6 were waited for; matrix products, arithmetic and copies ran while one was open for 12% of the time, Pallas kernels for 0%

commit v1 on v0

--- a/solution.py
+++ b/solution.py
@@ -93,7 +93,10 @@
         jnp.ones(state_shape, jnp.float32),
         jnp.zeros(state_shape + (HD,), jnp.float32),
     )
-    page_rows = lax.all_gather(prefix_cache, "req", axis=1, tiled=True)
+    page_rows = jnp.concatenate(
+        lax.all_to_all(jnp.stack([prefix_cache] * lax.axis_size("req"), axis=0), "req", 0, 0),
+        axis=1,
+    )
     span_rows = page_rows.shape[1]
     block_rows = 512
     chosen = page_rows[groups]

time: 791 us -> 763 us (0.965)
  waiting for transfers between devices: 203 us -> 173 us
  starting transfers between devices: 28 us -> 40.3 us
    all_gather x1 -> x0, waiting for transfers between devices: 56.3 us -> none  [body(): page_rows = lax.all_gather(prefix_cache, 'req', axis=1, tiled=True)]
    all_to_all x0 -> x1, waiting for transfers between devices: none -> 29.8 us  [body(): lax.all_to_all(jnp.stack([prefix_cache] * lax.axis_size('req'), axis=0),...]
    all_to_all x0 -> x1, starting transfers between devices: none -> 12.3 us  [body(): lax.all_to_all(jnp.stack([prefix_cache] * lax.axis_size('req'), axis=0),...]
    unnamed x4 -> x3, waiting for transfers between devices: 30.3 us -> 29.6 us
    unnamed x37 -> x38, local copies, waits for them, and re-layouts: 170 us -> 171 us
where the time goes in v1:
time: 763 us; the launch traced here: 755 us
  local copies, waits for them, and re-layouts  242 us (32%)
  blocking collectives  211 us (28%)
  waiting for transfers between devices  173 us (23%)
  starting transfers between devices  40.3 us (5%)
  matrix products  38.5 us (5%)
  other arithmetic  32 us (4%)
  between operations  14.1 us (2%)
    all_to_all x1, blocking collectives, body(): lax.all_to_all(rows_send, 'req', split_axis=0, concat_axis=0, tiled=True)  211 us
    unnamed x38, local copies, waits for them, and re-layouts  171 us
    all_to_all x1, waiting for transfers between devices, body(): lax.all_to_all(moved, 'req', split_axis=0, concat_axis=0, tiled=True)  55.5 us
    psum x1, waiting for transfers between devices, body(): residual = lax.psum((partial_value + placed).astype(jnp.bfloat16), 'tp')  41.3 us
    all_to_all x1, waiting for transfers between devices, body(): lax.all_to_all(jnp.stack([prefix_cache] * lax.axis_size('req'), axis=0),...  29.8 us
    unnamed x3, waiting for transfers between devices  29.6 us
  transfers between devices with their start and end apart: 7, of which 6 were waited for; matrix products, arithmetic and copies ran while one was open for 12% of the time, Pallas kernels for 0%

profile of v1, /device:TPU:2, one launch (start us, length us, event | category | flops | bytes accessed | tf_op | source)
XLA Modules:
  0.0 755.2 jit_solution(14975806135813404936)
XLA Ops:
  7.5 1.8 stack.2
  9.3 12.3 %all-to-all-start.3 = ((bf16[64,4,16,2,128]{4,2,3,1,0:T(8,128)(2,1)}), bf16[64,4,16,2,128]{4,2,3,1,0:T(8,128)(2,1)}, u32[]{:S(2)}, u32[]{:S(2)}) async-start(bf16[64,4,16,2,128]{4,2,3,1,0:T(8,128)(2,1)} %stack.2), calls=%async_computation.3 | async-start | bytes 4194304 | tf_op jit(solution)/shard_map/all_to_all | solution.py:97
  22.1 1.8 copy.79
  25.8 2.1 copy.80
  27.9 2.0 copy.82
  31.1 2.0 copy.83
  35.9 1.7 reduce-window.6
  40.6 2.4 fusion.60
  43.0 29.8 %all-to-all-done.3 = bf16[64,4,16,2,128]{4,2,3,1,0:T(8,128)(2,1)} async-done(((bf16[64,4,16,2,128]{4,2,3,1,0:T(8,128)(2,1)}), bf16[64,4,16,2,128]{4,2,3,1,0:T(8,128)(2,1)}, u32[]{:S(2)}, u32[]{:S(2)}) %all-to-all-start.3) | async-done | bytes 2097184 | tf_op jit(solution)/shard_map/all_to_all | solution.py:97
  72.8 3.3 copy.77
  76.0 4.6 gather_fusion.3
  80.7 14.7 %reshape.472 = bf16[8,2,512,2,2,64]{5,4,2,1,3,0:T(2,128)(2,1)} reshape(bf16[8,1024,2,128]{3,1,2,0:T(8,128)(2,1)} %gather_fusion.3) | data formatting | bytes 8388608 | tf_op jit(solution)/shard_map/reshape | solution.py:103
  95.4 20.0 %copy.84 = bf16[8,2,512,2,2,64]{2,5,4,0,3,1:T(8,128)(2,1)} copy(bf16[8,2,512,2,2,64]{5,4,2,1,3,0:T(2,128)(2,1)} %reshape.472) | data formatting | bytes 8388608
  115.5 26.8 %while.15 = (s32[]{:T(128)}, f32[8,16,2,8]{1,3,2,0:T(8,128)S(1)}, f32[8,16,2,8]{1,3,2,0:T(8,128)S(1)}, f32[8,16,2,8,64]{4,1,3,2,0:T(8,128)S(1)}, s32[2]{0:T(128)...) while((s32[]{:T(128)}, f32[8,16,2,8]{1,3,2,0:T(8,128)S(1)}, ...), condition=%wide.region_11.12_spmd.clone, body=%wide.region_8.11_spmd.clone.sunk | while | flops 277223424 | bytes 46792948 | solution.py:112
  118.2 1.9 dynamic-slice_bitcast_fusion.2
  122.2 1.9 copy-done.1
  125.4 3.4 fusion.76
  131.6 1.9 dynamic-slice_bitcast_fusion.2
  135.6 1.9 copy-done.1
  138.8 3.4 fusion.76
  142.3 1.6 fusion.38
  143.9 2.0 fusion.35
  146.5 4.4 fusion.61
  152.0 2.4 scatter_custom_fusion
  156.6 41.3 %all-reduce.3.cloned.1.call-done = bf16[128,2880]{0,1:T(8,128)(2,1)} async-done(((bf16[128,2880]{0,1:T(8,128)(2,1)}), bf16[128,2880]{0,1:T(8,128)(2,1)}) %all-reduce.3.cloned.1.call-update) | async-done | bytes 737296 | tf_op jit(solution)/shard_map/psum | solution.py:132
  197.9 2.3 copy.113
  201.3 8.1 %gather_fusion.4 = bf16[1536,2880]{1,0:T(8,128)(2,1)} fusion(bf16[129,2880]{1,0:T(8,128)(2,1)S(1)} %concatenate.27.clone, s32[2048]{0:T(1024)S(1)} %pad_clamp_fusion), kind=kCustom, calls=%fused_computation.4 | custom fusion | bytes 17700864 | tf_op jit(solution)/shard_map/gather | solution.py:165
  209.5 210.8 %all_to_all.30 = bf16[64,1,24,2880]{3,2,1,0:T(8,128)(2,1)S(1)} all-to-all(bf16[64,1,24,2880]{3,2,1,0:T(8,128)(2,1)} %bitcast.187), channel_id=1, replica_groups=mesh['req'=64,'tp'=4] {'req'}, dimensions={0} | all-to-all | bytes 17694720 | tf_op jit(solution)/shard_map/all_to_all | solution.py:175
  420.3 1.9 multiply_reduce_fusion
  423.7 10.1 %fusion.25 = f32[64,1,24,2,360]{4,2,3,0,1:T(8,128)S(1)} fusion(bf16[1,2880,2,360]{1,3,2,0:T(8,128)(2,1)} %param.28, f32[2880]{0:T(1024)S(1)} %copy-done.12, f32[64,24]{1,0:T(8,128)S(1)} %add_rsqrt_fusion, bf16[64,1,24,2880]{3,2,1,0:T(8,128)(2,1)S(1)} %all_to_all.30), kind=kOutput, calls=%fused_computation.40 | convolution fusion | flops 6387793920 | bytes 17435904 | tf_op jit(solution)/shard_map/njcd,jdgf->njcgf/dot_general | solution.py:181
  433.9 7.7 %convert_bitcast_fusion = bf16[64,1,24,2880]{3,2,0,1:T(8,128)(2,1)} fusion(bf16[1,360,2880]{2,1,0:T(8,128)(2,1)S(1)} %copy-done, f32[64,1,24,2,360]{4,2,3,0,1:T(8,128)S(1)} %fusion.25), kind=kOutput, calls=%fused_computation.31 | convolution fusion | flops 3192791040 | bytes 15344640 | tf_op jit(solution)/shard_map/njcf,jfd->njcd/dot_general | solution.py:185
  441.6 42.9 %copy.110 = bf16[64,1,24,2880]{2,0,1,3:T(8,128)(2,1)} copy(bf16[64,1,24,2880]{3,2,0,1:T(8,128)(2,1)} %convert_bitcast_fusion) | data formatting | bytes 17694720
  484.5 64.7 %reshape.473 = bf16[2880,1536]{1,0:T(8,128)(2,1)} reshape(bf16[2880,1,64,24]{3,2,1,0:T(8,128)(2,1)} %bitcast.185) | data formatting | bytes 17694720
  550.3 3.8 scatter_custom_fusion.1
  555.4 5.8 all-to-all-start.2
  561.3 8.5 %all-to-all-done.2 = bf16[64,1,24]{2,1,0:T(2,128)(2,1)S(1)} async-done(((bf16[64,1,24]{2,1,0:T(2,128)(2,1)}), bf16[64,1,24]{2,1,0:T(2,128)(2,1)S(1)}, u32[]{:S(2)}, u32[]{:S(2)}) %all-to-all-start.2) | async-done | bytes 3104 | tf_op jit(solution)/shard_map/all_to_all | solution.py:176
  569.8 5.5 all-to-all-start
  575.4 8.6 %all-to-all-done = s32[64,1,24]{2,1,0:T(1,128)S(1)} async-done(((s32[64,1,24]{2,1,0:T(1,128)}), s32[64,1,24]{2,1,0:T(1,128)S(1)}, u32[]{:S(2)}, u32[]{:S(2)}) %all-to-all-start) | async-done | bytes 6176 | tf_op jit(solution)/shard_map/all_to_all | solution.py:177
  585.2 5.9 all-to-all-start.1
  591.1 11.4 %convert_element_type.160 = f32[64,1,24,2880]{3,2,1,0:T(8,128)} convert(bf16[64,1,24,2880]{3,2,1,0:T(8,128)(2,1)} %copy-done.3) | non-fusion elementwise | flops 4423680 | bytes 26542080 | tf_op jit(solution)/shard_map/convert_element_type | solution.py:178
  602.5 29.6 %reduce-scatter.4.cloned.1.call-done = bf16[720,1536]{1,0:T(8,128)(2,1)} async-done(((bf16[2880,1536]{1,0:T(8,128)(2,1)}), bf16[720,1536]{1,0:T(8,128)(2,1)}) %reduce-scatter.4.cloned.1.call-update) | async-done | bytes 2211856
  632.1 21.0 %reshape.474 = bf16[720,1,64,24]{3,2,1,0:T(8,128)(2,1)} reshape(bf16[720,1536]{1,0:T(8,128)(2,1)} %reduce-scatter.4.cloned.1.call-done) | data formatting | bytes 4423680
  653.1 14.0 %copy.111 = bf16[64,1,24,720]{3,2,0,1:T(8,128)(2,1)} copy(bf16[64,1,24,720]{2,0,1,3:T(8,128)(2,1)} %bitcast.186) | data formatting | bytes 4423680
  667.1 6.4 fusion.23
  673.5 3.8 gather_fusion.5
  677.2 10.7 %all-to-all-start.5 = ((bf16[64,1,24,720]{3,2,1,0:T(8,128)(2,1)}), bf16[64,1,24,720]{3,2,1,0:T(8,128)(2,1)}, u32[]{:S(2)}, u32[]{:S(2)}) async-start(bf16[64,1,24,720]{3,2,1,0:T(8,128)(2,1)} %bitcast.189), calls=%async_computation.5 | async-start | bytes 4718592 | tf_op jit(solution)/shard_map/all_to_all | solution.py:198
  689.3 55.5 %all-to-all-done.5 = bf16[64,1,24,720]{3,2,1,0:T(8,128)(2,1)} async-done(((bf16[64,1,24,720]{3,2,1,0:T(8,128)(2,1)}), bf16[64,1,24,720]{3,2,1,0:T(8,128)(2,1)}, u32[]{:S(2)}, u32[]{:S(2)}) %all-to-all-start.5) | async-done | bytes 2211872 | tf_op jit(solution)/shard_map/all_to_all | solution.py:198
  744.7 3.4 convolution_convert_fusion
  (126 shorter events, 29.8 us)
Async XLA Ops:
  6.5 427.4 %copy-start = (bf16[1,360,2880]{2,1,0:T(8,128)(2,1)S(1)}, bf16[1,360,2880]{2,1,0:T(8,128)(2,1)}, u32[]{:S(2)}) copy-start(bf16[1,360,2880]{2,1,0:T(8,128)(2,1)} %param.29) | copy-start | bytes 6220804
  6.5 15.2 %copy-start.9 = (s32[128,4]{0,1:T(4,128)S(1)}, s32[128,4]{0,1:T(4,128)}, u32[]{:S(2)}) copy-start(s32[128,4]{0,1:T(4,128)} %param.24) | copy-start | bytes 6148
  9.3 23.8 %copy-start.6 = (bf16[128,2,128]{2,1,0:T(2,128)(2,1)S(1)}, bf16[128,2,128]{2,1,0:T(2,128)(2,1)}, u32[]{:S(2)}) copy-start(bf16[128,2,128]{2,1,0:T(2,128)(2,1)} %param.18) | copy-start | bytes 196612
  9.3 63.5 %all-to-all-start.3 = ((bf16[64,4,16,2,128]{4,2,3,1,0:T(8,128)(2,1)}), bf16[64,4,16,2,128]{4,2,3,1,0:T(8,128)(2,1)}, u32[]{:S(2)}, u32[]{:S(2)}) async-start(bf16[64,4,16,2,128]{4,2,3,1,0:T(8,128)(2,1)} %stack.2), calls=%async_computation.3 | async-start | bytes 4194304 | tf_op jit(solution)/shard_map/all_to_all | solution.py:97
  21.6 12.7 %copy-start.13 = (f32[16]{0:T(128)S(1)}, f32[16]{0:T(128)}, u32[]{:S(2)}) copy-start(f32[16]{0:T(128)} %param.20) | copy-start | bytes 196
  21.6 16.5 %copy-start.14 = (s32[8]{0:T(128)S(1)}, s32[8]{0:T(128)}, u32[]{:S(2)}) copy-start(s32[8]{0:T(128)} %param.22) | copy-start | bytes 100
  21.6 176.3 %all-reduce.3.cloned.1.call-start = ((), (), s32[]{:S(2)}) async-start(), calls=%async_computation.7 | async-start | bytes 1474560 | tf_op jit(solution)/shard_map/psum | solution.py:132
  22.1 17.6 %copy-start.15 = (s32[8]{0:T(128)S(1)}, s32[8]{0:T(128)}, u32[]{:S(2)}) copy-start(s32[8]{0:T(128)} %param.21) | copy-start | bytes 100
  39.8 0.8 copy-start.4
  39.9 0.6 copy-start.10
  118.2 3.2 copy-start.5
  120.1 1.3 copy-start.2
  122.2 1.9 copy-start.1
  131.6 3.2 copy-start.5
  133.5 1.3 copy-start.2
  135.6 1.9 copy-start.1
  146.4 4.4 copy-start.7
  151.9 480.2 %reduce-scatter.4.cloned.1.call-start = ((), (), s32[]{:S(2)}) async-start(), calls=%async_computation.8 | async-start | bytes 11059200
  420.3 3.4 copy-start.3
  420.3 3.4 copy-start.12
  549.2 0.6 copy-start.11
  549.2 0.7 copy-start.8
  549.2 12.0 %copy-start.16 = (s32[64]{0:T(128)S(1)}, s32[64]{0:T(128)}, u32[]{:S(2)}) copy-start(s32[64]{0:T(128)} %param.23) | copy-start | bytes 772
  555.4 14.4 %all-to-all-start.2 = ((bf16[64,1,24]{2,1,0:T(2,128)(2,1)}), bf16[64,1,24]{2,1,0:T(2,128)(2,1)S(1)}, u32[]{:S(2)}, u32[]{:S(2)}) async-start(bf16[64,1,24]{2,1,0:T(2,128)(2,1)} %copy.75), calls=%async_computation.2 | async-start | bytes 65536 | tf_op jit(solution)/shard_map/all_to_all | solution.py:176
  569.8 14.2 %all-to-all-start = ((s32[64,1,24]{2,1,0:T(1,128)}), s32[64,1,24]{2,1,0:T(1,128)S(1)}, u32[]{:S(2)}, u32[]{:S(2)}) async-start(s32[64,1,24]{2,1,0:T(1,128)} %bitcast.5), calls=%async_computation | async-start | bytes 65536 | tf_op jit(solution)/shard_map/all_to_all | solution.py:177
  585.2 92.1 %all-to-all-start.1 = ((s32[64,1,24]{2,1,0:T(1,128)}), s32[64,1,24]{2,1,0:T(1,128)S(1)}, u32[]{:S(2)}, u32[]{:S(2)}) async-start(s32[64,1,24]{2,1,0:T(1,128)} %bitcast.10), calls=%async_computation.1 | async-start | bytes 65536 | tf_op jit(solution)/shard_map/all_to_all | solution.py:199
  677.2 67.5 %all-to-all-start.5 = ((bf16[64,1,24,720]{3,2,1,0:T(8,128)(2,1)}), bf16[64,1,24,720]{3,2,1,0:T(8,128)(2,1)}, u32[]{:S(2)}, u32[]{:S(2)}) async-start(bf16[64,1,24,720]{3,2,1,0:T(8,128)(2,1)} %bitcast.189), calls=%async_computation.5 | async-start | bytes 4718592 | tf_op jit(solution)/shard_map/all_to_all | solution.py:198
Sparse Core Ops, SparseCore 0:
  152.0 45.8 all-reduce.2
  549.4 82.6 reduce-scatter.3
